TPU v7x, 128 devices: a whole 4x4x4 slice. The times are simulated.
128 devices in a mesh: dp: 8 (over z_hi, y), expert: 16 (over x, z_lo, core).
Axes of the slice: x: 4, y: 4, z: 4 (z_hi: 2, z_lo: 2; z = z_hi * 2 + z_lo), core: 2. Of those that a mesh axis runs over, the one named last changes fastest.
Arguments:
- tokens: bfloat16 [16384, 2880], P(('dp', 'expert')), may hold values from -6 to 6
- expert_ids: int32 [16384, 4], P(('dp', 'expert')), may hold values from 0 to 15, all different within a row; in each aligned block of 128 rows (0 to 127, 128 to 255, ...) at most 64 rows name the same one
- gates: bfloat16 [16384, 4], P(('dp', 'expert')), may hold values from 0.099609375 to 1
- w_gate: bfloat16 [16, 2880, 1440], P('expert'), may hold values from -0.109375 to 0.109375
- w_up: bfloat16 [16, 2880, 1440], P('expert'), may hold values from -0.109375 to 0.109375
- w_down: bfloat16 [16, 1440, 2880], P('expert'), may hold values from -0.15625 to 0.15625
Outputs:
- mixed: bfloat16 [16384, 2880], P(('dp', 'expert'))
- expert_load: int32 [16], replicated
Inputs may be any that keep to these rules, and one draw needn't show every extreme that they name: `expert_ids`: each token names 4 different experts. Among the rows of one device (aligned blocks of 128 rows) every expert is named by at most 64 rows, a bound that some block reaches.
All inputs are finite; a program needn't handle non-finite values.
Results may differ from a plain program's by a relative error of at most 0.004.
The roundings to bfloat16 on the way count: a program that leaves them out, or rounds other values in their place, can miss the bound.
Values may be sent and summed in bfloat16 or wider, within the bound.
No kernel may reach another device: no remote copies, remote signals or barrier semaphores. Data moves between devices by JAX's collectives and lax.ppermute only.
A program may use at most 192 MiB of HBM per device.

v0:
```python
import jax
import jax.numpy as jnp
from jax import lax
from jax.sharding import PartitionSpec as P

BLOCK = 128


def expert_ffn(rows, gate_mat, up_mat, down_mat):
    gate_val = jnp.dot(rows, gate_mat, preferred_element_type=jnp.float32)
    up_val = jnp.dot(rows, up_mat, preferred_element_type=jnp.float32)
    hidden = (jax.nn.silu(gate_val) * up_val).astype(jnp.bfloat16)
    return jnp.dot(hidden, down_mat, preferred_element_type=jnp.float32)


def shards(tokens, expert_ids, gates, w_gate, w_up, w_down):
    tok_rows = tokens.shape[0]
    width = tokens.shape[1]
    n_experts = lax.axis_size("expert")
    onehot = expert_ids[:, :, None] == jnp.arange(n_experts, dtype=jnp.int32)[None, None, :]
    table = jnp.sum(gates.astype(jnp.float32)[:, :, None] * onehot.astype(jnp.float32), axis=1)
    gate_mat = w_gate[0]
    up_mat = w_up[0]
    down_mat = w_down[0]
    gathered, table_all = (
        lax.all_gather(tokens, "expert", axis=0, tiled=True),
        lax.all_gather(table.astype(jnp.bfloat16), "expert", axis=0, tiled=True),
    )
    group_rows = gathered.shape[0]
    capacity = 8 * tok_rows
    expert = lax.axis_index("expert")
    column = lax.dynamic_index_in_dim(table_all, expert, 1, keepdims=False).astype(jnp.float32)
    routed = column > 0
    position = jnp.cumsum(routed.astype(jnp.int32)) - 1
    count = jnp.sum(routed.astype(jnp.int32))
    target = jnp.where(routed, position, capacity)
    slot_tok = (
        jnp.zeros((capacity,), jnp.int32)
        .at[target]
        .set(jnp.arange(group_rows, dtype=jnp.int32), mode="drop")
    )
    slot_weight = jnp.where(jnp.arange(capacity, dtype=jnp.int32) < count, column[slot_tok], 0.0)
    blocks = (count + BLOCK - 1) // BLOCK

    def per_block(index, partial_value):
        rows_idx = lax.dynamic_slice_in_dim(slot_tok, index * BLOCK, BLOCK)
        weight = lax.dynamic_slice_in_dim(slot_weight, index * BLOCK, BLOCK)
        result = expert_ffn(gathered[rows_idx], gate_mat, up_mat, down_mat)
        return partial_value.at[rows_idx].add(result * weight[:, None])

    partial_value = lax.fori_loop(0, blocks, per_block, jnp.zeros((group_rows, width), jnp.float32))
    mixed = lax.psum_scatter(partial_value, "expert", scatter_dimension=0, tiled=True).astype(
        jnp.bfloat16
    )
    local_load = jnp.sum(onehot.astype(jnp.float32), axis=(0, 1))
    expert_load = lax.psum(local_load, ("dp", "expert")).astype(jnp.int32)
    return (mixed, expert_load)


def solution(mesh):
    placed = (
        P(("dp", "expert"), None),
        P(("dp", "expert"), None),
        P(("dp", "expert"), None),
        P("expert", None, None),
        P("expert", None, None),
        P("expert", None, None),
    )
    return jax.shard_map(
        shards,
        mesh=mesh,
        in_specs=placed,
        out_specs=(P(("dp", "expert"), None), P()),
        check_vma=False,
    )
```

profile of v0, /device:TPU:1, one launch (start us, length us, event | category | flops | bytes accessed | tf_op | source)
XLA Modules:
  0.0 763.2 jit_solution(13569613881962175138)
XLA Ops:
  7.2 2.3 copy.22
  9.5 0.7 convert_element_type.40
  10.2 0.8 convert_reduce_fusion
  11.0 21.7 %all_gather.6 = bf16[2048,16]{0,1:T(8,128)(2,1)S(1)} all-gather(bf16[128,16]{0,1:T(8,128)(2,1)S(1)} %get-tuple-element.52), channel_id=1, replica_groups=mesh['dp'=8,'expert'=16] {'expert'}, dimensions={0}, use_global_device_ids=true | all-gather | bytes 69632 | tf_op jit(solution)/shard_map/all_gather | solution.py:27
  32.8 0.6 convert_reduce_fusion.1
  34.1 0.3 reduce-window.9
  34.4 0.1 slice.13
  34.5 0.1 slice_reduce_fusion
  34.6 0.1 add_add_fusion
  34.7 8.0 %scatter_custom_fusion.1 = s32[1024]{0:T(1024)S(1)} fusion(s32[2048]{0:T(1024)S(1)} %bitcast.30, s32[2048]{0:T(1024)S(1)} %iota.10, s32[]{:T(128)} %constant.29.clone.1), kind=kCustom, calls=%fused_computation.25 | custom fusion | bytes 4100 | tf_op jit(solution)/shard_map/scatter | solution.py:40
  42.8 6.2 gather_fusion.1
  48.9 11.9 %copy.23 = bf16[1,2880,1440]{2,1,0:T(8,128)(2,1)} copy(bf16[1,2880,1440]{1,2,0:T(8,128)(2,1)} %param.11) | data formatting | bytes 16588800 | tf_op args[3]
  60.8 11.9 %copy.24 = bf16[1,2880,1440]{2,1,0:T(8,128)(2,1)} copy(bf16[1,2880,1440]{1,2,0:T(8,128)(2,1)} %param.12) | data formatting | bytes 16588800 | tf_op args[4]
  72.7 0.6 fusion.4
  73.4 9.5 %all-gather.2.cloned.1.call-done = bf16[2048,2880]{1,0:T(8,128)(2,1)} async-done(((bf16[128,2880]{1,0:T(8,128)(2,1)}), bf16[2048,2880]{1,0:T(8,128)(2,1)}) %all-gather.2.cloned.1.call-update) | async-done | bytes 11796496 | tf_op jit(solution)/shard_map/all_gather | solution.py:26
  82.9 9.5 %broadcast_in_dim.23 = f32[2048,2880]{1,0:T(8,128)} broadcast(f32[]{:T(128)} %constant.30.clone.1), dimensions={} | broadcast | bytes 23592964 | tf_op jit(solution)/shard_map/broadcast_in_dim | solution.py:51
  92.4 386.5 %while.10 = (s32[]{:T(128)}, f32[2048,2880]{1,0:T(8,128)}, s32[]{:T(128)}, s32[1024]{0:T(1024)S(1)}, bf16[2048,2880]{1,0:T(8,128)(2,1)}, /*index=5*/bf16[2880,14...) while((s32[]{:T(128)}, f32[2048,2880]{1,0:T(8,128)}, ...), condition=%wide.region_7.8_spmd, body=%wide.region_5.7_spmd.sunk | while | flops 3186894336 | bytes 38162608 | solution.py:51
  92.6 7.8 %gather_fusion = bf16[128,2880]{1,0:T(8,128)(2,1)S(1)} fusion(bf16[2048,2880]{1,0:T(8,128)(2,1)} %get-tuple-element.159, s32[1024]{0:T(1024)S(1)} %pad_clamp_fusion.2), kind=kCustom, calls=%fused_computation.clone.1 | custom fusion | bytes 1475072 | tf_op jit(solution)/shard_map/while/body/gather | solution.py:48
  100.4 7.0 fusion.24
  107.3 14.5 %convolution_multiply_fusion.3 = f32[128,2880]{0,1:T(8,128)S(1)} fusion(bf16[1440,2880]{1,0:T(8,128)(2,1)} %get-tuple-element.162, f32[128]{0:T(128)S(1)} %dynamic_slice.17, bf16[128,2880]{1,0:T(8,128)(2,1)S(1)} %gather_fusion, bf16[2880,1440]{1,0:T(8,128)(2,1)} %get-tuple-element.161, f32[128,1440]{0,1:T(8,128)S(1)} %fusion.24), kind=kOutput, calls=%fused_computation.4.clone.1 | convolution fusion | flops 2124840960 | bytes 19538432 | tf_op jit(solution)/shard_map/while/body/dot_general | solution.py:13
  121.9 0.5 copy.27
  122.3 18.4 %scatter_fusion = f32[2048,2880]{1,0:T(8,128)} fusion(f32[2048,2880]{1,0:T(8,128)} %get-tuple-element.143, s32[128]{0:T(128)S(1)} %compare_select_fusion.5, f32[128,2880]{1,0:T(8,128)S(1)} %copy.27), kind=kCustom, calls=%fused_computation.2.clone.1 | custom fusion | flops 368640 | bytes 4424192 | tf_op jit(solution)/shard_map/while/body/scatter-add | solution.py:49
  140.9 7.8 %gather_fusion = bf16[128,2880]{1,0:T(8,128)(2,1)S(1)} fusion(bf16[2048,2880]{1,0:T(8,128)(2,1)} %get-tuple-element.159, s32[1024]{0:T(1024)S(1)} %pad_clamp_fusion.2), kind=kCustom, calls=%fused_computation.clone.1 | custom fusion | bytes 1475072 | tf_op jit(solution)/shard_map/while/body/gather | solution.py:48
  148.7 7.0 fusion.24
  155.7 14.5 %convolution_multiply_fusion.3 = f32[128,2880]{0,1:T(8,128)S(1)} fusion(bf16[1440,2880]{1,0:T(8,128)(2,1)} %get-tuple-element.162, f32[128]{0:T(128)S(1)} %dynamic_slice.17, bf16[128,2880]{1,0:T(8,128)(2,1)S(1)} %gather_fusion, bf16[2880,1440]{1,0:T(8,128)(2,1)} %get-tuple-element.161, f32[128,1440]{0,1:T(8,128)S(1)} %fusion.24), kind=kOutput, calls=%fused_computation.4.clone.1 | convolution fusion | flops 2124840960 | bytes 19538432 | tf_op jit(solution)/shard_map/while/body/dot_general | solution.py:13
  170.2 0.5 copy.27
  170.7 18.4 %scatter_fusion = f32[2048,2880]{1,0:T(8,128)} fusion(f32[2048,2880]{1,0:T(8,128)} %get-tuple-element.143, s32[128]{0:T(128)S(1)} %compare_select_fusion.5, f32[128,2880]{1,0:T(8,128)S(1)} %copy.27), kind=kCustom, calls=%fused_computation.2.clone.1 | custom fusion | flops 368640 | bytes 4424192 | tf_op jit(solution)/shard_map/while/body/scatter-add | solution.py:49
  189.2 7.8 %gather_fusion = bf16[128,2880]{1,0:T(8,128)(2,1)S(1)} fusion(bf16[2048,2880]{1,0:T(8,128)(2,1)} %get-tuple-element.159, s32[1024]{0:T(1024)S(1)} %pad_clamp_fusion.2), kind=kCustom, calls=%fused_computation.clone.1 | custom fusion | bytes 1475072 | tf_op jit(solution)/shard_map/while/body/gather | solution.py:48
  197.0 7.0 fusion.24
  204.0 14.5 %convolution_multiply_fusion.3 = f32[128,2880]{0,1:T(8,128)S(1)} fusion(bf16[1440,2880]{1,0:T(8,128)(2,1)} %get-tuple-element.162, f32[128]{0:T(128)S(1)} %dynamic_slice.17, bf16[128,2880]{1,0:T(8,128)(2,1)S(1)} %gather_fusion, bf16[2880,1440]{1,0:T(8,128)(2,1)} %get-tuple-element.161, f32[128,1440]{0,1:T(8,128)S(1)} %fusion.24), kind=kOutput, calls=%fused_computation.4.clone.1 | convolution fusion | flops 2124840960 | bytes 19538432 | tf_op jit(solution)/shard_map/while/body/dot_general | solution.py:13
  218.5 0.5 copy.27
  219.0 18.4 %scatter_fusion = f32[2048,2880]{1,0:T(8,128)} fusion(f32[2048,2880]{1,0:T(8,128)} %get-tuple-element.143, s32[128]{0:T(128)S(1)} %compare_select_fusion.5, f32[128,2880]{1,0:T(8,128)S(1)} %copy.27), kind=kCustom, calls=%fused_computation.2.clone.1 | custom fusion | flops 368640 | bytes 4424192 | tf_op jit(solution)/shard_map/while/body/scatter-add | solution.py:49
  237.4 0.1 compare_select_fusion.5
  237.5 7.8 %gather_fusion = bf16[128,2880]{1,0:T(8,128)(2,1)S(1)} fusion(bf16[2048,2880]{1,0:T(8,128)(2,1)} %get-tuple-element.159, s32[1024]{0:T(1024)S(1)} %pad_clamp_fusion.2), kind=kCustom, calls=%fused_computation.clone.1 | custom fusion | bytes 1475072 | tf_op jit(solution)/shard_map/while/body/gather | solution.py:48
  245.3 7.0 fusion.24
  252.3 14.5 %convolution_multiply_fusion.3 = f32[128,2880]{0,1:T(8,128)S(1)} fusion(bf16[1440,2880]{1,0:T(8,128)(2,1)} %get-tuple-element.162, f32[128]{0:T(128)S(1)} %dynamic_slice.17, bf16[128,2880]{1,0:T(8,128)(2,1)S(1)} %gather_fusion, bf16[2880,1440]{1,0:T(8,128)(2,1)} %get-tuple-element.161, f32[128,1440]{0,1:T(8,128)S(1)} %fusion.24), kind=kOutput, calls=%fused_computation.4.clone.1 | convolution fusion | flops 2124840960 | bytes 19538432 | tf_op jit(solution)/shard_map/while/body/dot_general | solution.py:13
  266.8 0.5 copy.27
  267.3 18.4 %scatter_fusion = f32[2048,2880]{1,0:T(8,128)} fusion(f32[2048,2880]{1,0:T(8,128)} %get-tuple-element.143, s32[128]{0:T(128)S(1)} %compare_select_fusion.5, f32[128,2880]{1,0:T(8,128)S(1)} %copy.27), kind=kCustom, calls=%fused_computation.2.clone.1 | custom fusion | flops 368640 | bytes 4424192 | tf_op jit(solution)/shard_map/while/body/scatter-add | solution.py:49
  285.7 0.1 compare_select_fusion.5
  285.9 7.8 %gather_fusion = bf16[128,2880]{1,0:T(8,128)(2,1)S(1)} fusion(bf16[2048,2880]{1,0:T(8,128)(2,1)} %get-tuple-element.159, s32[1024]{0:T(1024)S(1)} %pad_clamp_fusion.2), kind=kCustom, calls=%fused_computation.clone.1 | custom fusion | bytes 1475072 | tf_op jit(solution)/shard_map/while/body/gather | solution.py:48
  293.6 7.0 fusion.24
  300.6 14.5 %convolution_multiply_fusion.3 = f32[128,2880]{0,1:T(8,128)S(1)} fusion(bf16[1440,2880]{1,0:T(8,128)(2,1)} %get-tuple-element.162, f32[128]{0:T(128)S(1)} %dynamic_slice.17, bf16[128,2880]{1,0:T(8,128)(2,1)S(1)} %gather_fusion, bf16[2880,1440]{1,0:T(8,128)(2,1)} %get-tuple-element.161, f32[128,1440]{0,1:T(8,128)S(1)} %fusion.24), kind=kOutput, calls=%fused_computation.4.clone.1 | convolution fusion | flops 2124840960 | bytes 19538432 | tf_op jit(solution)/shard_map/while/body/dot_general | solution.py:13
  315.2 0.5 copy.27
  315.6 18.4 %scatter_fusion = f32[2048,2880]{1,0:T(8,128)} fusion(f32[2048,2880]{1,0:T(8,128)} %get-tuple-element.143, s32[128]{0:T(128)S(1)} %compare_select_fusion.5, f32[128,2880]{1,0:T(8,128)S(1)} %copy.27), kind=kCustom, calls=%fused_computation.2.clone.1 | custom fusion | flops 368640 | bytes 4424192 | tf_op jit(solution)/shard_map/while/body/scatter-add | solution.py:49
  334.2 7.8 %gather_fusion = bf16[128,2880]{1,0:T(8,128)(2,1)S(1)} fusion(bf16[2048,2880]{1,0:T(8,128)(2,1)} %get-tuple-element.159, s32[1024]{0:T(1024)S(1)} %pad_clamp_fusion.2), kind=kCustom, calls=%fused_computation.clone.1 | custom fusion | bytes 1475072 | tf_op jit(solution)/shard_map/while/body/gather | solution.py:48
  342.0 7.0 fusion.24
  348.9 14.5 %convolution_multiply_fusion.3 = f32[128,2880]{0,1:T(8,128)S(1)} fusion(bf16[1440,2880]{1,0:T(8,128)(2,1)} %get-tuple-element.162, f32[128]{0:T(128)S(1)} %dynamic_slice.17, bf16[128,2880]{1,0:T(8,128)(2,1)S(1)} %gather_fusion, bf16[2880,1440]{1,0:T(8,128)(2,1)} %get-tuple-element.161, f32[128,1440]{0,1:T(8,128)S(1)} %fusion.24), kind=kOutput, calls=%fused_computation.4.clone.1 | convolution fusion | flops 2124840960 | bytes 19538432 | tf_op jit(solution)/shard_map/while/body/dot_general | solution.py:13
  363.5 0.5 copy.27
  363.9 18.4 %scatter_fusion = f32[2048,2880]{1,0:T(8,128)} fusion(f32[2048,2880]{1,0:T(8,128)} %get-tuple-element.143, s32[128]{0:T(128)S(1)} %compare_select_fusion.5, f32[128,2880]{1,0:T(8,128)S(1)} %copy.27), kind=kCustom, calls=%fused_computation.2.clone.1 | custom fusion | flops 368640 | bytes 4424192 | tf_op jit(solution)/shard_map/while/body/scatter-add | solution.py:49
  382.5 7.8 %gather_fusion = bf16[128,2880]{1,0:T(8,128)(2,1)S(1)} fusion(bf16[2048,2880]{1,0:T(8,128)(2,1)} %get-tuple-element.159, s32[1024]{0:T(1024)S(1)} %pad_clamp_fusion.2), kind=kCustom, calls=%fused_computation.clone.1 | custom fusion | bytes 1475072 | tf_op jit(solution)/shard_map/while/body/gather | solution.py:48
  390.3 7.0 fusion.24
  397.3 14.5 %convolution_multiply_fusion.3 = f32[128,2880]{0,1:T(8,128)S(1)} fusion(bf16[1440,2880]{1,0:T(8,128)(2,1)} %get-tuple-element.162, f32[128]{0:T(128)S(1)} %dynamic_slice.17, bf16[128,2880]{1,0:T(8,128)(2,1)S(1)} %gather_fusion, bf16[2880,1440]{1,0:T(8,128)(2,1)} %get-tuple-element.161, f32[128,1440]{0,1:T(8,128)S(1)} %fusion.24), kind=kOutput, calls=%fused_computation.4.clone.1 | convolution fusion | flops 2124840960 | bytes 19538432 | tf_op jit(solution)/shard_map/while/body/dot_general | solution.py:13
  411.8 0.5 copy.27
  412.3 18.4 %scatter_fusion = f32[2048,2880]{1,0:T(8,128)} fusion(f32[2048,2880]{1,0:T(8,128)} %get-tuple-element.143, s32[128]{0:T(128)S(1)} %compare_select_fusion.5, f32[128,2880]{1,0:T(8,128)S(1)} %copy.27), kind=kCustom, calls=%fused_computation.2.clone.1 | custom fusion | flops 368640 | bytes 4424192 | tf_op jit(solution)/shard_map/while/body/scatter-add | solution.py:49
  430.8 7.8 %gather_fusion = bf16[128,2880]{1,0:T(8,128)(2,1)S(1)} fusion(bf16[2048,2880]{1,0:T(8,128)(2,1)} %get-tuple-element.159, s32[1024]{0:T(1024)S(1)} %pad_clamp_fusion.2), kind=kCustom, calls=%fused_computation.clone.1 | custom fusion | bytes 1475072 | tf_op jit(solution)/shard_map/while/body/gather | solution.py:48
  438.6 7.0 fusion.24
  445.6 14.5 %convolution_multiply_fusion.3 = f32[128,2880]{0,1:T(8,128)S(1)} fusion(bf16[1440,2880]{1,0:T(8,128)(2,1)} %get-tuple-element.162, f32[128]{0:T(128)S(1)} %dynamic_slice.17, bf16[128,2880]{1,0:T(8,128)(2,1)S(1)} %gather_fusion, bf16[2880,1440]{1,0:T(8,128)(2,1)} %get-tuple-element.161, f32[128,1440]{0,1:T(8,128)S(1)} %fusion.24), kind=kOutput, calls=%fused_computation.4.clone.1 | convolution fusion | flops 2124840960 | bytes 19538432 | tf_op jit(solution)/shard_map/while/body/dot_general | solution.py:13
  460.1 0.5 copy.27
  460.6 18.4 %scatter_fusion = f32[2048,2880]{1,0:T(8,128)} fusion(f32[2048,2880]{1,0:T(8,128)} %get-tuple-element.143, s32[128]{0:T(128)S(1)} %compare_select_fusion.5, f32[128,2880]{1,0:T(8,128)S(1)} %copy.27), kind=kCustom, calls=%fused_computation.2.clone.1 | custom fusion | flops 368640 | bytes 4424192 | tf_op jit(solution)/shard_map/while/body/scatter-add | solution.py:49
  479.0 23.9 %copy.25 = f32[2048,2880]{0,1:T(8,128)} copy(f32[2048,2880]{1,0:T(8,128)} %get-tuple-element.50) | data formatting | bytes 47185920 | tf_op jit(solution)/shard_map/while | solution.py:51
  502.9 105.1 %psum.7 = f32[16]{0:T(128)S(1)} all-reduce(f32[16]{0:T(128)S(1)} %get-tuple-element.51), channel_id=1, replica_groups=mesh['dp'=8,'expert'=16] {'dp','expert'}, use_global_device_ids=true, to_apply=%region_10.11 | all-reduce | flops 16 | bytes 128 | tf_op jit(solution)/shard_map/psum | solution.py:56
  608.0 0.5 convert_element_type.50
  608.5 145.5 %reduce-scatter.2.cloned.1.call-done = f32[128,2880]{0,1:T(8,128)} async-done(((f32[2048,2880]{0,1:T(8,128)}), f32[128,2880]{0,1:T(8,128)}) %reduce-scatter.2.cloned.1.call-update) | async-done | bytes 1474576 | tf_op jit(solution)/shard_map/reduce_scatter | solution.py:52
  754.0 2.3 convert_element_type.48
  (31 shorter events, 1.3 us)
Async XLA Ops:
  7.2 75.7 %all-gather.2.cloned.1.call-start = ((), (), s32[]{:S(2)}) async-start(), calls=%async_computation.1 | async-start | bytes 12812288 | tf_op jit(solution)/shard_map/all_gather | solution.py:26
  9.5 744.6 %reduce-scatter.2.cloned.1.call-start = ((), (), s32[]{:S(2)}) async-start(), calls=%async_computation.2 | async-start | bytes 25067520 | tf_op jit(solution)/shard_map/reduce_scatter | solution.py:52
Sparse Core Ops, SparseCore 0:
  9.7 73.1 all-gather.1
  503.0 250.9 reduce-scatter.1
where the time goes:
time: 765 us; the launch traced here: 763 us
  matrix products  172 us (22%)
  waiting for transfers between devices  155 us (20%)
  other arithmetic  154 us (20%)
  local copies, waits for them, and re-layouts  140 us (18%)
  blocking collectives  127 us (17%)
  between operations  14.8 us (2%)
    scatter-add x8, other arithmetic, per_block(): return partial_value.at[rows_idx].add(result * weight[:, None])  147 us
    reduce_scatter x1, waiting for transfers between devices, shards(): lax.psum_scatter(partial_value, 'expert', scatter_dimension=0, tiled=True)  146 us
    dot_general x8, matrix products, expert_ffn(): return jnp.dot(hidden, down_mat, preferred_element_type=jnp.float32)  116 us
    psum x1, blocking collectives, shards(): expert_load = lax.psum(local_load, ('dp', 'expert')).astype(jnp.int32)  105 us
    gather x8, local copies, waits for them, and re-layouts, per_block(): result = expert_ffn(gathered[rows_idx], gate_mat, up_mat, down_mat)  62.3 us
    dot_general x8, matrix products, expert_ffn(): gate_val = jnp.dot(rows, gate_mat, preferred_element_type=jnp.float32)  55.7 us
    unnamed x3, local copies, waits for them, and re-layouts  26 us
    while x1, local copies, waits for them, and re-layouts, shards(): lax.fori_loop(0, blocks, per_block, jnp.zeros((group_rows, width), jnp.fl...  23.9 us
  transfers between devices with their start and end apart: 2, of which 2 were waited for; matrix products, arithmetic and copies ran while one was open for 5% of the time, Pallas kernels for 0%

commit v1 on v0

v1 whole, which is shorter than its diff:
```python
import jax
import jax.numpy as jnp
from jax import lax
from jax.sharding import PartitionSpec as P

SRC_CAP = 64


def split3(value):
    hi = value.astype(jnp.bfloat16)
    rest = value - hi.astype(jnp.float32)
    mid = rest.astype(jnp.bfloat16)
    lo = (rest - mid.astype(jnp.float32)).astype(jnp.bfloat16)
    return hi, mid, lo


def shards(tokens, expert_ids, gates, w_gate, w_up, w_down):
    tok_rows, width = tokens.shape
    n_experts = lax.axis_size("expert")
    cap = SRC_CAP
    experts = jnp.arange(n_experts, dtype=jnp.int32)
    onehot = expert_ids[:, :, None] == experts[None, None, :]
    routed = jnp.any(onehot, axis=1)
    position = jnp.cumsum(routed.astype(jnp.int32), axis=0) - 1
    slots = jnp.arange(cap, dtype=jnp.int32)
    pick = routed.T[:, None, :] & (position.T[:, None, :] == slots[None, :, None])
    pick = pick.reshape(n_experts * cap, tok_rows)
    send = jnp.dot(pick.astype(jnp.bfloat16), tokens, preferred_element_type=jnp.float32)
    send = send.astype(jnp.bfloat16).reshape(n_experts, cap, width)
    rows = lax.all_to_all(send, "expert", 0, 0, tiled=True).reshape(n_experts * cap, width)

    gate_val = jnp.dot(rows, w_gate[0], preferred_element_type=jnp.float32)
    up_val = jnp.dot(rows, w_up[0], preferred_element_type=jnp.float32)
    hidden = (jax.nn.silu(gate_val) * up_val).astype(jnp.bfloat16)
    result = jnp.dot(hidden, w_down[0], preferred_element_type=jnp.float32)

    back = lax.all_to_all(result.reshape(n_experts, cap, width), "expert", 0, 0, tiled=True)
    back = back.reshape(n_experts * cap, width)
    table = jnp.sum(gates.astype(jnp.float32)[:, :, None] * onehot.astype(jnp.float32), axis=1)
    weight = jnp.where(pick.T.reshape(tok_rows, n_experts, cap), table[:, :, None], 0.0)
    weight = weight.reshape(tok_rows, n_experts * cap).astype(jnp.bfloat16)
    mixed = sum(
        jnp.dot(weight, piece, preferred_element_type=jnp.float32) for piece in split3(back)
    ).astype(jnp.bfloat16)

    local_load = jnp.sum(onehot.astype(jnp.int32), axis=(0, 1))
    expert_load = lax.psum(local_load, ("dp", "expert"))
    return (mixed, expert_load)


def solution(mesh):
    placed = (
        P(("dp", "expert"), None),
        P(("dp", "expert"), None),
        P(("dp", "expert"), None),
        P("expert", None, None),
        P("expert", None, None),
        P("expert", None, None),
    )
    return jax.shard_map(
        shards,
        mesh=mesh,
        in_specs=placed,
        out_specs=(P(("dp", "expert"), None), P()),
        check_vma=False,
    )
```

time: 765 us -> 416 us (0.54)
  blocking collectives: 127 us -> 325 us
  waiting for transfers between devices: 155 us -> 0.01 us
  other arithmetic: 154 us -> 16.9 us
  local copies, waits for them, and re-layouts: 140 us -> 13.4 us
  matrix products: 172 us -> 54.7 us
  between operations: 14.8 us -> 0.77 us
    scatter-add x8 -> x0, other arithmetic: 147 us -> none  [per_block(): return partial_value.at[rows_idx].add(result * weight[:, None])]
    reduce_scatter x1 -> x0, waiting for transfers between devices: 146 us -> none  [shards(): lax.psum_scatter(partial_value, 'expert', scatter_dimension=0, tiled=True)]
    psum x1, blocking collectives: 105 us -> 248 us  [shards(): expert_load = lax.psum(local_load, ('dp', 'expert'))]
    dot_general x16 -> x7, matrix products: 172 us -> 54.7 us  [the longest x1 15.9 us: shards(): result = jnp.dot(hidden, w_down[0], preferred_element_type=jnp.float32)]
    all_to_all x0 -> x1, blocking collectives: none -> 76.6 us  [shards(): lax.all_to_all(send, 'expert', 0, 0, tiled=True)]
    gather x9 -> x0, local copies, waits for them, and re-layouts: 68.5 us -> none  [the longest x8 62.3 us: per_block(): result = expert_ffn(gathered[rows_idx], gate_mat, up_mat, down_mat)]
    unnamed x3 -> x20, local copies, waits for them, and re-layouts: 26 us -> 0.05 us
    while x1 -> x0, local copies, waits for them, and re-layouts: 23.9 us -> none  [shards(): lax.fori_loop(0, blocks, per_block, jnp.zeros((group_rows, width), jnp.fl...]
  transfers between devices with their start and end apart: 2 -> 1, of which waited for: 2 -> 0; matrix products, arithmetic and copies ran while one was open for 5% -> 0% of each run, Pallas kernels for 0% -> 0%
where the time goes in v1:
time: 416 us
  blocking collectives  325 us (78%)
  matrix products  54.7 us (13%)
  other arithmetic  16.9 us (4%)
  local copies, waits for them, and re-layouts  13.4 us (3%)
  starting transfers between devices  5.17 us (1%)
    psum x1, blocking collectives, shards(): expert_load = lax.psum(local_load, ('dp', 'expert'))  248 us
    all_to_all x1, blocking collectives, shards(): lax.all_to_all(send, 'expert', 0, 0, tiled=True)  76.6 us
    dot_general x1, matrix products, shards(): result = jnp.dot(hidden, w_down[0], preferred_element_type=jnp.float32)  15.9 us
    dot_general x1, matrix products, shards(): up_val = jnp.dot(rows, w_up[0], preferred_element_type=jnp.float32)  11.9 us
    dot_general x1, matrix products, shards(): gate_val = jnp.dot(rows, w_gate[0], preferred_element_type=jnp.float32)  11.5 us
    dot_general x3, matrix products, shards(): jnp.dot(weight, piece, preferred_element_type=jnp.float32)  11.1 us
    convert_element_type x1, other arithmetic, split3(): lo = (rest - mid.astype(jnp.float32)).astype(jnp.bfloat16)  10.3 us
    convert_element_type x1, local copies, waits for them, and re-layouts, shards(): send = send.astype(jnp.bfloat16).reshape(n_experts, cap, width)  8.51 us
  transfers between devices with their start and end apart: 1, of which 0 were waited for; matrix products, arithmetic and copies ran while one was open for 0% of the time, Pallas kernels for 0%

profile of v1, /device:TPU:1, one launch (start us, length us, event | category | flops | bytes accessed | tf_op | source)
XLA Modules:
  0.0 415.8 jit_solution(15631615467178035169)
XLA Ops:
  0.6 0.0 copy-start
  0.6 0.8 fusion.12
  1.4 0.1 copy.19
  1.5 0.2 reduce_window_sum.11
  1.7 0.1 copy.20
  1.8 0.1 eq.39
  1.8 0.2 fusion.11
  2.1 0.0 copy-done
  2.1 4.3 %convolution_convert_fusion = bf16[1024,2880]{0,1:T(8,128)(2,1)} fusion(pred[1024,128]{1,0:T(32,128)(4,1)S(1)} %fusion.11, bf16[128,2880]{0,1:T(8,128)(2,1)S(1)} %copy-done), kind=kOutput, calls=%fused_computation.11 | convolution fusion | flops 757923840 | bytes 6766592 | tf_op jit(solution)/shard_map/dot_general | solution.py:28
  6.3 8.5 %copy.21 = bf16[1024,2880]{1,0:T(8,128)(2,1)} copy(bf16[1024,2880]{0,1:T(8,128)(2,1)} %convolution_convert_fusion) | data formatting | bytes 11796480 | tf_op jit(solution)/shard_map/convert_element_type | solution.py:29
  14.9 0.0 slice-start
  14.9 76.6 %all_to_all.10 = bf16[16,64,2880]{2,1,0:T(8,128)(2,1)S(1)} all-to-all(bf16[16,64,2880]{2,1,0:T(8,128)(2,1)} %bitcast.58), channel_id=1, replica_groups=mesh['dp'=8,'expert'=16] {'expert'}, dimensions={0} | all-to-all | bytes 11796480 | tf_op jit(solution)/shard_map/all_to_all | solution.py:30
  91.4 0.0 slice-start.1
  91.4 0.0 slice-start.2
  91.4 11.9 %fusion.2 = f32[1024,1440]{0,1:T(8,128)S(1)} fusion(bf16[1024,2880]{1,0:T(8,128)(2,1)S(1)} %bitcast.59, bf16[1,2880,1440]{1,2,0:T(8,128)(2,1)} %param.10), kind=kOutput, calls=%fused_computation.5 | convolution fusion | flops 8493465600 | bytes 20090880 | tf_op jit(solution)/shard_map/dot_general | solution.py:33
  103.3 0.0 slice-done
  103.3 0.0 slice-done.1
  103.3 0.0 slice-done.2
  103.4 11.5 %multiply_convert_fusion = bf16[1024,1440]{0,1:T(8,128)(2,1)} fusion(f32[1024,1440]{0,1:T(8,128)S(1)} %fusion.2, bf16[1024,2880]{1,0:T(8,128)(2,1)S(1)} %bitcast.60, bf16[1,2880,1440]{1,2,0:T(8,128)(2,1)S(1)} %bitcast.65), kind=kOutput, calls=%fused_computation.10 | convolution fusion | flops 8502312960 | bytes 23040000 | tf_op jit(solution)/shard_map/dot_general | solution.py:32
  114.8 4.6 %copy.22 = bf16[1024,1440]{1,0:T(8,128)(2,1)} copy(bf16[1024,1440]{0,1:T(8,128)(2,1)} %multiply_convert_fusion) | data formatting | bytes 5898240 | tf_op jit(solution)/shard_map/convert_element_type | solution.py:34
  119.4 15.9 %fusion = f32[16,64,2880]{2,1,0:T(8,128)} fusion(bf16[16,64,1440]{2,1,0:T(8,128)(2,1)} %bitcast.61, bf16[1,1440,2880]{2,1,0:T(8,128)(2,1)} %param.11), kind=kOutput, calls=%fused_computation.3 | convolution fusion | flops 8493465600 | bytes 23040000 | tf_op jit(solution)/shard_map/dot_general | solution.py:35
  135.4 0.0 copy-start.5
  135.4 0.0 copy-start.6
  135.4 5.2 %all-to-all-start.1 = ((f32[16,64,2880]{2,1,0:T(8,128)}), f32[16,64,2880]{2,1,0:T(8,128)}, u32[]{:S(2)}, u32[]{:S(2)}) async-start(f32[16,64,2880]{2,1,0:T(8,128)} %fusion), calls=%async_computation.1 | async-start | bytes 24117248 | tf_op jit(solution)/shard_map/all_to_all | solution.py:37
  140.5 0.0 copy-done.5
  140.6 0.1 convert_reduce_fusion
  140.7 248.3 %psum.7 = s32[16]{0:T(128)} all-reduce(s32[16]{0:T(128)S(1)} %convert_reduce_fusion), channel_id=1, replica_groups=mesh['dp'=8,'expert'=16] {'dp','expert'}, use_global_device_ids=true, to_apply=%region_4.5 | all-reduce | flops 16 | bytes 128 | tf_op jit(solution)/shard_map/psum | solution.py:47
  388.9 0.0 copy-done.6
  389.0 0.2 fusion.10
  389.2 0.0 copy-start.3
  389.2 0.0 all-to-all-done.1
  389.2 5.1 %bitcast_convert_fusion = bf16[1024,2880]{1,0:T(8,128)(2,1)S(1)} fusion(f32[16,64,2880]{2,1,0:T(8,128)} %all-to-all-done.1), kind=kLoop, calls=%fused_computation.1 | loop fusion | flops 2949120 | bytes 17694720 | tf_op jit(solution)/shard_map/convert_element_type | solution.py:10
  394.3 0.0 copy-done.3
  394.3 2.5 fusion.13
  396.9 0.0 copy-start.4
  396.9 10.3 %subtract_convert_fusion = (bf16[1024,2880]{1,0:T(8,128)(2,1)}, bf16[1024,2880]{1,0:T(8,128)(2,1)}) fusion(f32[16,64,2880]{2,1,0:T(8,128)} %all-to-all-done.1), kind=kLoop, calls=%fused_computation.2 | loop fusion | flops 20643840 | bytes 23592960 | tf_op jit(solution)/shard_map/convert_element_type | solution.py:13
  407.2 0.0 copy-start.2
  407.2 0.0 copy-done.4
  407.2 0.0 copy-start.1
  407.2 5.3 %convolution_add_fusion.1 = f32[128,2880]{0,1:T(8,128)S(1)} fusion(f32[128,2880]{0,1:T(8,128)S(1)} %fusion.13, bf16[128,1024]{0,1:T(8,128)(2,1)S(1)} %copy-done.4, bf16[1024,2880]{1,0:T(8,128)(2,1)} %get-tuple-element.3), kind=kOutput, calls=%fused_computation.13 | convolution fusion | flops 755343360 | bytes 9109504 | tf_op jit(solution)/shard_map/dot_general | solution.py:43
  412.5 0.0 copy-done.2
  412.5 3.3 fusion.9
  415.8 0.0 copy-done.1
  (6 shorter events, 0.0 us)
Async XLA Ops:
  0.6 1.4 copy-start
  14.9 88.5 %slice-start = ((s8[8478720]{0:T(1024)(128)(4,1)}), s8[4194304]{0:T(1024)(128)(4,1)S(1)}, s32[]{:S(2)}) async-start(s8[8478720]{0:T(1024)(128)(4,1)} %bitcast.64), calls=%async_computation.2 | async-start | bytes 8388608
  91.4 11.9 %slice-start.1 = ((s8[8478720]{0:T(1024)(128)(4,1)}), s8[4194304]{0:T(1024)(128)(4,1)S(1)}, s32[]{:S(2)}) async-start(s8[8478720]{0:T(1024)(128)(4,1)} %bitcast.64), calls=%async_computation.3 | async-start | bytes 8388608
  91.4 11.9 %slice-start.2 = ((s8[8478720]{0:T(1024)(128)(4,1)}), s8[90112]{0:T(1024)(128)(4,1)S(1)}, s32[]{:S(2)}) async-start(s8[8478720]{0:T(1024)(128)(4,1)} %bitcast.64), calls=%async_computation.4 | async-start | bytes 180224
  135.4 5.2 %copy-start.5 = (s32[128,4]{0,1:T(4,128)S(1)}, s32[128,4]{0,1:T(4,128)}, u32[]{:S(2)}) copy-start(s32[128,4]{0,1:T(4,128)} %param.7) | copy-start | bytes 6148
  135.4 253.6 %copy-start.6 = (bf16[128,4]{0,1:T(4,128)(2,1)S(1)}, bf16[128,4]{0,1:T(4,128)(2,1)}, u32[]{:S(2)}) copy-start(bf16[128,4]{0,1:T(4,128)(2,1)} %param.8) | copy-start | bytes 3076
  135.4 253.8 %all-to-all-start.1 = ((f32[16,64,2880]{2,1,0:T(8,128)}), f32[16,64,2880]{2,1,0:T(8,128)}, u32[]{:S(2)}, u32[]{:S(2)}) async-start(f32[16,64,2880]{2,1,0:T(8,128)} %fusion), calls=%async_computation.1 | async-start | bytes 24117248 | tf_op jit(solution)/shard_map/all_to_all | solution.py:37
  389.2 5.1 %copy-start.3 = (bf16[128,1024]{0,1:T(8,128)(2,1)}, bf16[128,1024]{0,1:T(8,128)(2,1)S(1)}, u32[]{:S(2)}) copy-start(bf16[128,1024]{0,1:T(8,128)(2,1)S(1)} %fusion.10) | copy-start | bytes 786436
  396.9 10.3 %copy-start.4 = (bf16[128,1024]{0,1:T(8,128)(2,1)S(1)}, bf16[128,1024]{0,1:T(8,128)(2,1)}, u32[]{:S(2)}) copy-start(bf16[128,1024]{0,1:T(8,128)(2,1)} %copy-done.3) | copy-start | bytes 786436
  407.2 5.3 %copy-start.2 = (bf16[1024,2880]{1,0:T(8,128)(2,1)S(1)}, bf16[1024,2880]{1,0:T(8,128)(2,1)}, u32[]{:S(2)}) copy-start(bf16[1024,2880]{1,0:T(8,128)(2,1)} %get-tuple-element.2) | copy-start | bytes 17694724
  407.2 8.6 %copy-start.1 = (bf16[128,2880]{0,1:T(8,128)(2,1)S(1)}, bf16[128,2880]{0,1:T(8,128)(2,1)}, u32[]{:S(2)}) copy-start(bf16[128,2880]{0,1:T(8,128)(2,1)} %param.6) | copy-start | bytes 2211844
